TPU v7x, 32 devices: a whole 2x2x4 slice. The times are simulated.
32 devices in a mesh: illum: 8 (over z, y), tile: 4 (over x, core).
Axes of the slice: x: 2, y: 2, z: 4, core: 2. Of those that a mesh axis runs over, the one named last changes fastest.
Arguments:
- tilts: int32 [8, 2], P('illum'), may hold values from -64 to 64
- taps: float32 [2, 33], replicated, may hold values from -0.75 to 0.75
- stored_planes: float32 [2, 128, 4096], P(None, 'tile', 'illum'), may hold values from -3.140625 to 3.140625
- owner: int32 [2, 8], replicated, may hold values from 0 to 7, each once within a row
Outputs:
- exit_field: float32 [2, 8, 128, 4096], P(None, 'illum', 'tile')
Inputs may be any that keep to these rules, and one draw needn't show every extreme that they name: Each row of owner is a permutation of the 8 stored column blocks.
All inputs are finite; a program needn't handle non-finite values.
Results may differ from a plain program's by a relative error of at most 0.0003.
Values sent between devices are 32-bit elements; how exact they have to be, the bound alone decides.
No kernel may reach another device: no remote copies, remote signals or barrier semaphores. Data moves between devices by JAX's collectives and lax.ppermute only.
A program may use at most 64 MiB of HBM per device.

v0:
```python
import jax
import jax.numpy as jnp
from jax import lax
from jax.sharding import PartitionSpec as P

NY = 4096
PLANES = 2
HALF = 16
two_pi = 6.283185307179586


def extended(cells, sides, width):
    for axis, dim in sides:
        count = lax.axis_size(axis)
        ends = count - 1
        head = lax.slice_in_dim(cells, 0, width, axis=dim)
        tail = lax.slice_in_dim(cells, cells.shape[dim] - width, cells.shape[dim], axis=dim)
        cells = jnp.concatenate(
            [
                lax.ppermute(tail, axis, [(i, (i + 1) % count) for i in range(ends)]),
                cells,
                lax.ppermute(head, axis, [((i + 1) % count, i) for i in range(ends)]),
            ],
            axis=dim,
        )
    return cells


def toeplitz(tap_row, block):
    rows = jnp.arange(block + 2 * HALF)[:, None]
    cols = jnp.arange(block)[None, :]
    offset = rows - cols
    steps = jnp.arange(2 * HALF + 1)
    return jnp.sum(jnp.where(offset[:, :, None] == steps, tap_row, 0.0), axis=2)


def band_matrix(tap_row, count):
    rows = jnp.arange(count)[:, None]
    cols = jnp.arange(count + 2 * HALF)[None, :]
    offset = cols - rows
    steps = jnp.arange(2 * HALF + 1)
    return jnp.sum(jnp.where(offset[:, :, None] == steps, tap_row, 0.0), axis=2)


def windows(field, block):
    length = field.shape[-1]
    count = length // block
    widths = [(0, 0)] * (field.ndim - 1) + [(HALF, block - HALF)]
    padded = jnp.pad(field, widths)
    lead = field.shape[:-1]
    main = padded[..., :length].reshape(lead + (count, block))
    after = padded[..., block : length + block].reshape(lead + (count, block))[..., : 2 * HALF]
    return jnp.concatenate([main, after], axis=-1)


def along_pass(real, imag, taps):
    block = min(128, real.shape[-1])
    win_real = windows(real, block)
    win_imag = windows(imag, block)
    kern_real = toeplitz(taps[0], block)
    kern_imag = toeplitz(taps[1], block)

    def apply(win, kern):
        out = jnp.einsum("...nj,jc->...nc", win, kern, precision=lax.Precision.HIGHEST)
        return out.reshape(real.shape)

    return (
        apply(win_real, kern_real) - apply(win_imag, kern_imag),
        apply(win_real, kern_imag) + apply(win_imag, kern_real),
    )


def cross_pass(real, imag, taps):
    count = real.shape[1] - 2 * HALF
    band_real = band_matrix(taps[0], count)
    band_imag = band_matrix(taps[1], count)

    def apply(band, field):
        return jnp.einsum("ij,ajy->aiy", band, field, precision=lax.Precision.HIGHEST)

    return (
        apply(band_real, real) - apply(band_imag, imag),
        apply(band_real, imag) + apply(band_imag, real),
    )


def transmit(real, imag, screen):
    cosine = jnp.cos(screen)
    sine = jnp.sin(screen)
    return (real * cosine - imag * sine, real * sine + imag * cosine)


def reorder(gathered, owner):
    count = gathered.shape[1]
    blocks = owner.shape[1]
    width = gathered.shape[2] // blocks
    planes = [
        gathered[p].reshape(count, blocks, width)[:, owner[p], :].reshape(count, blocks * width)
        for p in range(gathered.shape[0])
    ]
    return jnp.stack(planes)


def body(tilts, taps, stored_planes, owner):
    local_rows = stored_planes.shape[1]
    total_rows = local_rows * lax.axis_size("tile")
    total_cols = NY
    first_row = lax.axis_index("tile") * local_rows
    gathered = lax.all_gather(stored_planes, "illum", axis=2, tiled=True)
    screens = reorder(gathered, owner)
    extra = 0
    span = local_rows + 2 * extra
    global_rows = first_row - extra + jnp.arange(span, dtype=jnp.int32)
    inside = (global_rows >= 0) & (global_rows < total_rows)
    cols = jnp.arange(total_cols, dtype=jnp.int32)
    across = (
        jnp.mod(tilts[:, 0:1] * global_rows[None, :], total_rows).astype(jnp.float32) / total_rows
    )
    along = jnp.mod(tilts[:, 1:2] * cols[None, :], total_cols).astype(jnp.float32) / total_cols
    theta = two_pi * (across[:, :, None] + along[:, None, :])
    real = jnp.where(inside[None, :, None], jnp.cos(theta), 0.0)
    imag = jnp.where(inside[None, :, None], jnp.sin(theta), 0.0)
    for plane in range(PLANES):
        real, imag = transmit(real, imag, screens[plane])
        packed = extended(jnp.stack([real, imag]), (("tile", 2),), HALF)
        real, imag = cross_pass(packed[0], packed[1], taps)
        real, imag = along_pass(real, imag, taps)
    return jnp.stack([real, imag])


def solution(mesh):
    in_specs = (P("illum", None), P(), P(None, "tile", "illum"), P())
    out_specs = P(None, "illum", "tile", None)
    return jax.shard_map(body, mesh=mesh, in_specs=in_specs, out_specs=out_specs, check_vma=False)
```

profile of v0, /device:TPU:1, one launch (start us, length us, event | category | flops | bytes accessed | tf_op | source)
XLA Modules:
  0.0 116.0 jit_solution(4339684245039347680)
XLA Ops:
  6.5 0.7 all-gather.2.cloned.1.call-update
  7.3 1.4 %fusion.42 = (s32[1,1]{1,0:T(1,128)}, s32[1,1]{1,0:T(1,128)}) fusion(s32[1,2]{1,0:T(1,128)} %param.4), kind=kLoop, calls=%fused_computation.110 | loop fusion | bytes 16 | tf_op jit(solution)/shard_map/slice | solution.py:117
  9.3 0.8 fusion.32
  10.1 0.7 fusion.24
  10.8 0.8 slice_bitcast_fusion.20
  11.8 39.1 %all-gather.2.cloned.1.call-done = f32[2,32,4096]{2,1,0:T(8,128)} async-done(((f32[2,32,512]{2,1,0:T(8,128)}), f32[2,32,4096]{2,1,0:T(8,128)}) %all-gather.2.cloned.1.call-update) | async-done | bytes 1048592 | tf_op jit(solution)/shard_map/all_gather | solution.py:109
  50.9 1.3 %fusion.41 = (f32[1,32,4096]{2,1,0:T(8,128)S(1)}, f32[1,32,4096]{2,1,0:T(8,128)S(1)}) fusion(f32[2,32,4096]{2,1,0:T(8,128)} %all-gather.2.cloned.1.call-done), kind=kLoop, calls=%fused_computation.109 | loop fusion | bytes 2097152 | tf_op jit(solution)/shard_map/slice | solution.py:98
  53.4 1.9 %sine_bitcast_fusion.1 = (f32[32,8,512]{2,0,1:T(8,128)S(1)}, f32[32,8,512]{2,0,1:T(8,128)S(1)}) fusion(f32[8,32,512]{2,1,0:T(8,128)S(1)} %gather_fusion), kind=kLoop, calls=%fused_computation.49 | loop fusion | bytes 1572864 | tf_op jit(solution)/shard_map/sin | solution.py:89
  56.1 2.2 %multiply_subtract_fusion.1 = (f32[1,1,32,4096]{3,2,1,0:T(8,128)S(1)}, f32[1,1,32,4096]{3,2,1,0:T(8,128)S(1)}) fusion(f32[1,1,32,4096]{3,2,1,0:T(8,128)S(1)} %sin.57, f32[1,1,32,4096]{3,2,1,0:T(8,128)S(1)} %cos.57, f32[4096]{0:T(1024)S(1)} %fusion.24, f32[32]{0:T(128)S(1)} %fusion.29, pred[32]{0:T(512)(128)(4,1)S(1)} %compare_and_fusion), kind=kLoop, calls=%fused_computation.62 | loop fusion | flops 1310720 | bytes 2113696 | tf_op jit(solution)/shard_map/sub | solution.py:90
  58.2 0.9 fusion.13
  59.1 4.6 %collective-permute-start = (f32[2,1,16,4096]{3,2,1,0:T(8,128)}, f32[2,1,16,4096]{3,2,1,0:T(8,128)}, u32[]{:S(2)}, u32[]{:S(2)}) collective-permute-start(f32[2,1,16,4096]{3,2,1,0:T(8,128)} %get-tuple-element.17), channel_id=1, source_target_pairs={{0,1},{1,2},{2,3},{4,5},{5,6},{6,7},{8,9},{9,10},{10,11},{12,13},{... | collective-permute-start | bytes 1572872 | tf_op jit(solution)/shard_map/ppermute | solution.py:20
  63.8 2.1 %collective-permute-start.1 = (f32[2,1,16,4096]{3,2,1,0:T(8,128)S(1)}, f32[2,1,16,4096]{3,2,1,0:T(8,128)}, u32[]{:S(2)}, u32[]{:S(2)}) collective-permute-start(f32[2,1,16,4096]{3,2,1,0:T(8,128)S(1)} %get-tuple-element.18), channel_id=1, source_target_pairs={{1,0},{2,1},{3,2},{5,4},{6,5},{7,6},{9,8},{10,9},{11,10},{13,12},{... | collective-permute-start | bytes 1572872 | tf_op jit(solution)/shard_map/ppermute | solution.py:22
  67.7 1.9 %sine_bitcast_fusion = (f32[32,8,512]{2,0,1:T(8,128)S(1)}, f32[32,8,512]{2,0,1:T(8,128)S(1)}) fusion(f32[8,32,512]{2,1,0:T(8,128)S(1)} %gather_fusion.1), kind=kLoop, calls=%fused_computation.47 | loop fusion | bytes 1572864 | tf_op jit(solution)/shard_map/sin | solution.py:89
  70.4 4.0 %collective-permute-done.1 = f32[2,1,16,4096]{3,2,1,0:T(8,128)} collective-permute-done((f32[2,1,16,4096]{3,2,1,0:T(8,128)S(1)}, f32[2,1,16,4096]{3,2,1,0:T(8,128)}, u32[]{:S(2)}, u32[]{:S(2)}) %collective-permute-start.1) | collective-permute-done | bytes 524320 | tf_op jit(solution)/shard_map/ppermute | solution.py:22
  74.4 1.3 %pad_maximum_fusion = f32[2,1,64,4096]{3,2,1,0:T(8,128)S(1)} fusion(f32[2,1,16,4096]{3,2,1,0:T(8,128)} %collective-permute-done.1, f32[1,1,32,4096]{3,2,1,0:T(8,128)S(1)} %get-tuple-element.12, f32[1,1,32,4096]{3,2,1,0:T(8,128)S(1)} %get-tuple-element.11, f32[2,1,16,4096]{3,2,1,0:T(8,128)} %collective-permute-done), kind=kLoop, calls=%fused_computation.13 | loop fusion | flops 1572864 | bytes 4194304 | tf_op jit(solution)/shard_map/concatenate | solution.py:18
  77.1 0.7 fusion
  78.3 0.7 fusion.1
  79.6 1.0 fusion.11
  80.5 1.0 fusion.10
  81.5 1.8 %convolution_subtract_fusion.3 = f32[32,32,128]{2,1,0:T(8,128)} fusion(f32[32,32,128]{2,1,0:T(8,128)S(1)} %fusion.11, f32[1,32,32,32]{3,2,1,0:T(8,128)S(1)} %bitcast.154, f32[1,32,32,128]{3,2,1,0:T(8,128)S(1)} %bitcast.156, f32[160,128]{1,0:T(8,128)S(1)} %get-tuple-element.6), kind=kOutput, calls=%fused_computation.18 | convolution fusion | flops 251953152 | bytes 1785856 | tf_op jit(solution)/shard_map/...nj,jc->...nc/dot_general | solution.py:64
  83.3 1.1 sub.176
  84.4 1.8 %convolution_add_fusion.3 = f32[32,32,128]{2,1,0:T(8,128)} fusion(f32[32,32,128]{2,1,0:T(8,128)S(1)} %fusion.10, f32[1,32,32,32]{3,2,1,0:T(8,128)S(1)} %bitcast.155, f32[1,32,32,128]{3,2,1,0:T(8,128)S(1)} %bitcast.157, f32[160,128]{1,0:T(8,128)S(1)} %get-tuple-element.5), kind=kOutput, calls=%fused_computation.17 | convolution fusion | flops 251953152 | bytes 1785856 | tf_op jit(solution)/shard_map/...nj,jc->...nc/dot_general | solution.py:64
  86.2 1.1 add.184
  87.5 1.9 %collective-permute-start.2 = (f32[2,1,16,4096]{3,2,1,0:T(8,128)S(1)}, f32[2,1,16,4096]{3,2,1,0:T(8,128)S(1)}, u32[]{:S(2)}, u32[]{:S(2)}) collective-permute-start(f32[2,1,16,4096]{3,2,1,0:T(8,128)S(1)} %get-tuple-element.13), channel_id=1, source_target_pairs={{0,1},{1,2},{2,3},{4,5},{5,6},{6,7},{8,9},{9,10},{10,11},{12,13},{... | collective-permute-start | bytes 1572872 | tf_op jit(solution)/shard_map/ppermute | solution.py:20
  89.5 2.7 %collective-permute-start.3 = (f32[2,1,16,4096]{3,2,1,0:T(8,128)S(1)}, f32[2,1,16,4096]{3,2,1,0:T(8,128)S(1)}, u32[]{:S(2)}, u32[]{:S(2)}) collective-permute-start(f32[2,1,16,4096]{3,2,1,0:T(8,128)S(1)} %get-tuple-element.14), channel_id=1, source_target_pairs={{1,0},{2,1},{3,2},{5,4},{6,5},{7,6},{9,8},{10,9},{11,10},{13,12},{... | collective-permute-start | bytes 1572872 | tf_op jit(solution)/shard_map/ppermute | solution.py:22
  92.1 3.4 %collective-permute-done.2 = f32[2,1,16,4096]{3,2,1,0:T(8,128)S(1)} collective-permute-done((f32[2,1,16,4096]{3,2,1,0:T(8,128)S(1)}, f32[2,1,16,4096]{3,2,1,0:T(8,128)S(1)}, u32[]{:S(2)}, u32[]{:S(2)}) %collective-permute-start.2) | collective-permute-done | bytes 524320 | tf_op jit(solution)/shard_map/ppermute | solution.py:20
  95.6 4.4 %collective-permute-done.3 = f32[2,1,16,4096]{3,2,1,0:T(8,128)S(1)} collective-permute-done((f32[2,1,16,4096]{3,2,1,0:T(8,128)S(1)}, f32[2,1,16,4096]{3,2,1,0:T(8,128)S(1)}, u32[]{:S(2)}, u32[]{:S(2)}) %collective-permute-start.3) | collective-permute-done | bytes 524320 | tf_op jit(solution)/shard_map/ppermute | solution.py:22
  102.8 1.0 fusion.9
  103.7 1.0 fusion.8
  105.9 1.0 convolution_subtract_fusion.2
  107.0 1.0 convolution_add_fusion.2
  108.1 1.0 pad_maximum_fusion.2
  (46 shorter events, 12.2 us)
Async XLA Ops:
  6.5 44.3 %all-gather.2.cloned.1.call-start = ((), (), s32[]{:S(2)}) async-start(), calls=%async_computation | async-start | bytes 1179648 | tf_op jit(solution)/shard_map/all_gather | solution.py:109
  59.1 11.3 %collective-permute-start = (f32[2,1,16,4096]{3,2,1,0:T(8,128)}, f32[2,1,16,4096]{3,2,1,0:T(8,128)}, u32[]{:S(2)}, u32[]{:S(2)}) collective-permute-start(f32[2,1,16,4096]{3,2,1,0:T(8,128)} %get-tuple-element.17), channel_id=1, source_target_pairs={{0,1},{1,2},{2,3},{4,5},{5,6},{6,7},{8,9},{9,10},{10,11},{12,13},{... | collective-permute-start | bytes 1572872 | tf_op jit(solution)/shard_map/ppermute | solution.py:20
  63.8 10.6 %collective-permute-start.1 = (f32[2,1,16,4096]{3,2,1,0:T(8,128)S(1)}, f32[2,1,16,4096]{3,2,1,0:T(8,128)}, u32[]{:S(2)}, u32[]{:S(2)}) collective-permute-start(f32[2,1,16,4096]{3,2,1,0:T(8,128)S(1)} %get-tuple-element.18), channel_id=1, source_target_pairs={{1,0},{2,1},{3,2},{5,4},{6,5},{7,6},{9,8},{10,9},{11,10},{13,12},{... | collective-permute-start | bytes 1572872 | tf_op jit(solution)/shard_map/ppermute | solution.py:22
  87.5 8.0 %collective-permute-start.2 = (f32[2,1,16,4096]{3,2,1,0:T(8,128)S(1)}, f32[2,1,16,4096]{3,2,1,0:T(8,128)S(1)}, u32[]{:S(2)}, u32[]{:S(2)}) collective-permute-start(f32[2,1,16,4096]{3,2,1,0:T(8,128)S(1)} %get-tuple-element.13), channel_id=1, source_target_pairs={{0,1},{1,2},{2,3},{4,5},{5,6},{6,7},{8,9},{9,10},{10,11},{12,13},{... | collective-permute-start | bytes 1572872 | tf_op jit(solution)/shard_map/ppermute | solution.py:20
  89.5 10.5 %collective-permute-start.3 = (f32[2,1,16,4096]{3,2,1,0:T(8,128)S(1)}, f32[2,1,16,4096]{3,2,1,0:T(8,128)S(1)}, u32[]{:S(2)}, u32[]{:S(2)}) collective-permute-start(f32[2,1,16,4096]{3,2,1,0:T(8,128)S(1)} %get-tuple-element.14), channel_id=1, source_target_pairs={{1,0},{2,1},{3,2},{5,4},{6,5},{7,6},{9,8},{10,9},{11,10},{13,12},{... | collective-permute-start | bytes 1572872 | tf_op jit(solution)/shard_map/ppermute | solution.py:22
Sparse Core Ops, SparseCore 0:
  9.5 41.2 all-gather.1
where the time goes:
time: 116 us
  waiting for transfers between devices  51.6 us (44%)
  local copies, waits for them, and re-layouts  15.7 us (14%)
  matrix products  14.8 us (13%)
  between operations  13.8 us (12%)
  starting transfers between devices  11.3 us (10%)
  other arithmetic  8.69 us (7%)
    all_gather x1, waiting for transfers between devices, body(): gathered = lax.all_gather(stored_planes, 'illum', axis=2, tiled=True)  39.1 us
    dot_general x8, matrix products, apply(): jnp.einsum('...nj,jc->...nc', win, kern, precision=lax.Precision.HIGHEST)  9.36 us
    ppermute x2, waiting for transfers between devices, extended(): lax.ppermute(head, axis, [((i + 1) % count, i) for i in range(ends)])  8.37 us
    ppermute x2, starting transfers between devices, extended(): lax.ppermute(tail, axis, [(i, (i + 1) % count) for i in range(ends)])  6.56 us
    dot_general x8, matrix products, apply(): jnp.einsum('ij,ajy->aiy', band, field, precision=lax.Precision.HIGHEST)  5.44 us
    ppermute x2, starting transfers between devices, extended(): lax.ppermute(head, axis, [((i + 1) % count, i) for i in range(ends)])  4.76 us
    sin x6, local copies, waits for them, and re-layouts, transmit(): sine = jnp.sin(screen)  4.53 us
    ppermute x2, waiting for transfers between devices, extended(): lax.ppermute(tail, axis, [(i, (i + 1) % count) for i in range(ends)])  3.44 us
  transfers between devices with their start and end apart: 5, of which 4 were waited for; matrix products, arithmetic and copies ran while one was open for 8% of the time, Pallas kernels for 0%

commit v1 on v0

--- a/solution.py
+++ b/solution.py
@@ -7,6 +7,28 @@
 PLANES = 2
 HALF = 16
 two_pi = 6.283185307179586
+
+
+def joined_along(blocks, dim):
+    shape = list(blocks.shape[1:])
+    shape[dim] *= blocks.shape[0]
+    return jnp.moveaxis(blocks, 0, dim).reshape(shape)
+
+
+def gather_around(x, axis, dim):
+    size = lax.axis_size(axis)
+    pairs = [(i, (i + 1) % size) for i in range(size)]
+    back = [(b, a) for a, b in pairs]
+    lower, upper = ([], [])
+    for step in range(size - 1):
+        if step % 2 == 0:
+            lower.append(lax.ppermute(lower[-1] if lower else x, axis, pairs))
+        else:
+            upper.append(lax.ppermute(upper[-1] if upper else x, axis, back))
+    blocks = jnp.stack([*lower[::-1], x, *upper])
+    shift = lax.axis_index(axis) - len(lower)
+    blocks = blocks[(jnp.arange(size) - shift) % size]
+    return joined_along(blocks, dim)
 
 
 def extended(cells, sides, width):
@@ -106,7 +128,7 @@
     total_rows = local_rows * lax.axis_size("tile")
     total_cols = NY
     first_row = lax.axis_index("tile") * local_rows
-    gathered = lax.all_gather(stored_planes, "illum", axis=2, tiled=True)
+    gathered = gather_around(stored_planes, "illum", 2)
     screens = reorder(gathered, owner)
     extra = 0
     span = local_rows + 2 * extra

time: 116 us -> 89.5 us (0.77)
  waiting for transfers between devices: 51.6 us -> 20.2 us
  starting transfers between devices: 11.3 us -> 29.7 us
  between operations: 13.8 us -> 0.49 us
    all_gather x1 -> x0, waiting for transfers between devices: 39.1 us -> none  [body(): gathered = lax.all_gather(stored_planes, 'illum', axis=2, tiled=True)]
    ppermute x0 -> x7, starting transfers between devices: none -> 14 us  [the longest x3 11.9 us: gather_around(): upper.append(lax.ppermute(upper[-1] if upper else x, axis, back))]
    ppermute x0 -> x7, waiting for transfers between devices: none -> 9.75 us  [the longest x4 9.06 us: gather_around(): lower.append(lax.ppermute(lower[-1] if lower else x, axis, pairs))]
    ppermute x2, starting transfers between devices: 6.56 us -> 11.6 us  [extended(): lax.ppermute(tail, axis, [(i, (i + 1) % count) for i in range(ends)])]
    ppermute x2, waiting for transfers between devices: 3.44 us -> 1.61 us  [extended(): lax.ppermute(tail, axis, [(i, (i + 1) % count) for i in range(ends)])]
    slice x1 -> x0, local copies, waits for them, and re-layouts: 1.27 us -> none  [reorder(): gathered[p].reshape(count, blocks, width)[:, owner[p], :]]
    unnamed x14 -> x19, local copies, waits for them, and re-layouts: 2.72 us -> 3.09 us
  transfers between devices with their start and end apart: 5 -> 11, of which waited for: 4 -> 9; matrix products, arithmetic and copies ran while one was open for 8% -> 10% of each run, Pallas kernels for 0% -> 0%
where the time goes in v1:
time: 89.5 us; the launch traced here: 88.7 us
  starting transfers between devices  29.7 us (33%)
  waiting for transfers between devices  20.2 us (23%)
  local copies, waits for them, and re-layouts  14.9 us (17%)
  matrix products  14.8 us (17%)
  other arithmetic  8.65 us (10%)
    ppermute x3, starting transfers between devices, gather_around(): upper.append(lax.ppermute(upper[-1] if upper else x, axis, back))  11.9 us
    ppermute x2, starting transfers between devices, extended(): lax.ppermute(tail, axis, [(i, (i + 1) % count) for i in range(ends)])  11.6 us
    dot_general x8, matrix products, apply(): jnp.einsum('...nj,jc->...nc', win, kern, precision=lax.Precision.HIGHEST)  9.37 us
    ppermute x4, waiting for transfers between devices, gather_around(): lower.append(lax.ppermute(lower[-1] if lower else x, axis, pairs))  9.06 us
    ppermute x2, waiting for transfers between devices, extended(): lax.ppermute(head, axis, [((i + 1) % count, i) for i in range(ends)])  8.89 us
    dot_general x8, matrix products, apply(): jnp.einsum('ij,ajy->aiy', band, field, precision=lax.Precision.HIGHEST)  5.44 us
    sin x6, local copies, waits for them, and re-layouts, transmit(): sine = jnp.sin(screen)  4.53 us
    ppermute x2, starting transfers between devices, extended(): lax.ppermute(head, axis, [((i + 1) % count, i) for i in range(ends)])  4.02 us
  transfers between devices with their start and end apart: 11, of which 9 were waited for; matrix products, arithmetic and copies ran while one was open for 10% of the time, Pallas kernels for 0%

profile of v1, /device:TPU:1, one launch (start us, length us, event | category | flops | bytes accessed | tf_op | source)
XLA Modules:
  0.0 88.7 jit_solution(4689435248343151030)
XLA Ops:
  0.0 2.1 %collective-permute-start = (f32[2,32,512]{2,1,0:T(8,128)}, f32[2,32,512]{2,1,0:T(8,128)S(1)}, u32[]{:S(2)}, u32[]{:S(2)}) collective-permute-start(f32[2,32,512]{2,1,0:T(8,128)} %param.6), channel_id=1, source_target_pairs={{0,4},{4,8},{8,12},{12,16},{16,20},{20,24},{24,28},{28,0},{1,5},{5... | collective-permute-start | bytes 393224 | tf_op jit(solution)/shard_map/ppermute | solution.py:25
  2.1 3.0 %collective-permute-start.4 = (f32[2,32,512]{2,1,0:T(8,128)}, f32[2,32,512]{2,1,0:T(8,128)S(1)}, u32[]{:S(2)}, u32[]{:S(2)}) collective-permute-start(f32[2,32,512]{2,1,0:T(8,128)} %param.6), channel_id=1, source_target_pairs={{4,0},{8,4},{12,8},{16,12},{20,16},{24,20},{28,24},{0,28},{5,1},{9... | collective-permute-start | bytes 393224 | tf_op jit(solution)/shard_map/ppermute | solution.py:27
  5.9 1.3 %fusion.43 = (s32[1,1]{1,0:T(1,128)}, s32[1,1]{1,0:T(1,128)}) fusion(s32[1,2]{1,0:T(1,128)} %param.4), kind=kLoop, calls=%fused_computation.127 | loop fusion | bytes 16 | tf_op jit(solution)/shard_map/slice | solution.py:139
  8.6 6.5 %collective-permute-done.1 = f32[2,32,512]{2,1,0:T(8,128)S(1)} collective-permute-done((f32[2,32,512]{2,1,0:T(8,128)S(1)}, f32[2,32,512]{2,1,0:T(8,128)S(1)}, u32[]{:S(2)}, u32[]{:S(2)}) %collective-permute-start.1) | collective-permute-done | bytes 131104 | tf_op jit(solution)/shard_map/ppermute | solution.py:25
  16.4 4.2 %collective-permute-start.5 = (f32[2,32,512]{2,1,0:T(8,128)S(1)}, f32[2,32,512]{2,1,0:T(8,128)S(1)}, u32[]{:S(2)}, u32[]{:S(2)}) collective-permute-start(f32[2,32,512]{2,1,0:T(8,128)S(1)} %collective-permute-done.4), channel_id=1, source_target_pairs={{4,0},{8,4},{12,8},{16,12},{20,16},{24,20},{28,24},{0,28},{5,1},{9... | collective-permute-start | bytes 393224 | tf_op jit(solution)/shard_map/ppermute | solution.py:27
  20.6 1.1 %collective-permute-done.2 = f32[2,32,512]{2,1,0:T(8,128)S(1)} collective-permute-done((f32[2,32,512]{2,1,0:T(8,128)S(1)}, f32[2,32,512]{2,1,0:T(8,128)S(1)}, u32[]{:S(2)}, u32[]{:S(2)}) %collective-permute-start.2) | collective-permute-done | bytes 131104 | tf_op jit(solution)/shard_map/ppermute | solution.py:25
  22.5 4.7 %collective-permute-start.6 = (f32[2,32,512]{2,1,0:T(8,128)S(1)}, f32[2,32,512]{2,1,0:T(8,128)S(1)}, u32[]{:S(2)}, u32[]{:S(2)}) collective-permute-start(f32[2,32,512]{2,1,0:T(8,128)S(1)} %collective-permute-done.5), channel_id=1, source_target_pairs={{4,0},{8,4},{12,8},{16,12},{20,16},{24,20},{28,24},{0,28},{5,1},{9... | collective-permute-start | bytes 393224 | tf_op jit(solution)/shard_map/ppermute | solution.py:27
  27.2 1.0 %collective-permute-done.3 = f32[2,32,512]{2,1,0:T(8,128)S(1)} collective-permute-done((f32[2,32,512]{2,1,0:T(8,128)S(1)}, f32[2,32,512]{2,1,0:T(8,128)S(1)}, u32[]{:S(2)}, u32[]{:S(2)}) %collective-permute-start.3) | collective-permute-done | bytes 131104 | tf_op jit(solution)/shard_map/ppermute | solution.py:25
  28.2 0.9 %bitcast_dynamic-update-slice_fusion.3 = f32[8,2,32,512]{3,2,1,0:T(8,128)S(1)} fusion(f32[8,2,32,512]{3,2,1,0:T(8,128)S(1)} %bitcast_dynamic-update-slice_fusion.4, f32[2,32,512]{2,1,0:T(8,128)} %param.6), kind=kLoop, calls=%fused_computation.72 | loop fusion | bytes 262144
  30.5 1.9 %sine_bitcast_fusion.1 = (f32[32,8,512]{2,0,1:T(8,128)S(1)}, f32[32,8,512]{2,0,1:T(8,128)S(1)}) fusion(f32[8,32,512]{2,1,0:T(8,128)S(1)} %gather_fusion.1), kind=kLoop, calls=%fused_computation.52 | loop fusion | bytes 1572864 | tf_op jit(solution)/shard_map/sin | solution.py:111
  33.3 2.2 %multiply_subtract_fusion.1 = (f32[1,1,32,4096]{3,2,1,0:T(8,128)S(1)}, f32[1,1,32,4096]{3,2,1,0:T(8,128)S(1)}) fusion(f32[1,1,32,4096]{3,2,1,0:T(8,128)S(1)} %sin.57, f32[1,1,32,4096]{3,2,1,0:T(8,128)S(1)} %cos.57, f32[4096]{0:T(1024)S(1)} %fusion.24, f32[32]{0:T(128)S(1)} %fusion.29, pred[32]{0:T(512)(128)(4,1)S(1)} %compare_and_fusion), kind=kLoop, calls=%fused_computation.65 | loop fusion | flops 1310720 | bytes 2113696 | tf_op jit(solution)/shard_map/sub | solution.py:112
  35.4 0.9 fusion.13
  36.3 7.8 %collective-permute-start.7 = (f32[2,1,16,4096]{3,2,1,0:T(8,128)}, f32[2,1,16,4096]{3,2,1,0:T(8,128)}, u32[]{:S(2)}, u32[]{:S(2)}) collective-permute-start(f32[2,1,16,4096]{3,2,1,0:T(8,128)} %get-tuple-element.17), channel_id=1, source_target_pairs={{0,1},{1,2},{2,3},{4,5},{5,6},{6,7},{8,9},{9,10},{10,11},{12,13},{... | collective-permute-start | bytes 1572872 | tf_op jit(solution)/shard_map/ppermute | solution.py:42
  44.1 2.1 %collective-permute-start.8 = (f32[2,1,16,4096]{3,2,1,0:T(8,128)S(1)}, f32[2,1,16,4096]{3,2,1,0:T(8,128)}, u32[]{:S(2)}, u32[]{:S(2)}) collective-permute-start(f32[2,1,16,4096]{3,2,1,0:T(8,128)S(1)} %get-tuple-element.18), channel_id=1, source_target_pairs={{1,0},{2,1},{3,2},{5,4},{6,5},{7,6},{9,8},{10,9},{11,10},{13,12},{... | collective-permute-start | bytes 1572872 | tf_op jit(solution)/shard_map/ppermute | solution.py:44
  47.4 1.9 %sine_bitcast_fusion = (f32[32,8,512]{2,0,1:T(8,128)S(1)}, f32[32,8,512]{2,0,1:T(8,128)S(1)}) fusion(f32[8,32,512]{2,1,0:T(8,128)S(1)} %gather_fusion.2), kind=kLoop, calls=%fused_computation.50 | loop fusion | bytes 1572864 | tf_op jit(solution)/shard_map/sin | solution.py:111
  50.5 4.2 %collective-permute-done.8 = f32[2,1,16,4096]{3,2,1,0:T(8,128)} collective-permute-done((f32[2,1,16,4096]{3,2,1,0:T(8,128)S(1)}, f32[2,1,16,4096]{3,2,1,0:T(8,128)}, u32[]{:S(2)}, u32[]{:S(2)}) %collective-permute-start.8) | collective-permute-done | bytes 524320 | tf_op jit(solution)/shard_map/ppermute | solution.py:44
  54.7 1.3 %pad_maximum_fusion = f32[2,1,64,4096]{3,2,1,0:T(8,128)S(1)} fusion(f32[2,1,16,4096]{3,2,1,0:T(8,128)} %collective-permute-done.8, f32[1,1,32,4096]{3,2,1,0:T(8,128)S(1)} %get-tuple-element.12, f32[1,1,32,4096]{3,2,1,0:T(8,128)S(1)} %get-tuple-element.11, f32[2,1,16,4096]{3,2,1,0:T(8,128)} %collective-permute-done.7), kind=kLoop, calls=%fused_computation.14 | loop fusion | flops 1572864 | bytes 4194304 | tf_op jit(solution)/shard_map/concatenate | solution.py:40
  59.9 1.0 %fusion.11 = f32[32,32,128]{2,1,0:T(8,128)S(1)} fusion(f32[1,32,32,32]{3,2,1,0:T(8,128)S(1)} %bitcast.163, f32[1,32,32,128]{3,2,1,0:T(8,128)S(1)} %bitcast.165, f32[160,128]{1,0:T(8,128)S(1)} %get-tuple-element.5), kind=kOutput, calls=%fused_computation.40 | convolution fusion | flops 251822080 | bytes 1261568 | tf_op jit(solution)/shard_map/...nj,jc->...nc/dot_general | solution.py:86
  60.9 1.0 %fusion.10 = f32[32,32,128]{2,1,0:T(8,128)S(1)} fusion(f32[1,32,32,32]{3,2,1,0:T(8,128)S(1)} %bitcast.164, f32[1,32,32,128]{3,2,1,0:T(8,128)S(1)} %bitcast.166, f32[160,128]{1,0:T(8,128)S(1)} %get-tuple-element.6), kind=kOutput, calls=%fused_computation.39 | convolution fusion | flops 251822080 | bytes 1261568 | tf_op jit(solution)/shard_map/...nj,jc->...nc/dot_general | solution.py:86
  61.8 1.8 %convolution_subtract_fusion.3 = f32[32,32,128]{2,1,0:T(8,128)} fusion(f32[32,32,128]{2,1,0:T(8,128)S(1)} %fusion.11, f32[1,32,32,32]{3,2,1,0:T(8,128)S(1)} %bitcast.171, f32[1,32,32,128]{3,2,1,0:T(8,128)S(1)} %bitcast.173, f32[160,128]{1,0:T(8,128)S(1)} %get-tuple-element.6), kind=kOutput, calls=%fused_computation.19 | convolution fusion | flops 251953152 | bytes 1785856 | tf_op jit(solution)/shard_map/...nj,jc->...nc/dot_general | solution.py:86
  63.6 1.1 %sub.195 = f32[1,1,32,4096]{3,2,1,0:T(8,128)S(1)} reshape(f32[32,32,128]{2,1,0:T(8,128)} %convolution_subtract_fusion.3) | data formatting | bytes 1048576 | tf_op jit(solution)/shard_map/sub | solution.py:90
  64.7 1.8 %convolution_add_fusion.3 = f32[32,32,128]{2,1,0:T(8,128)} fusion(f32[32,32,128]{2,1,0:T(8,128)S(1)} %fusion.10, f32[1,32,32,32]{3,2,1,0:T(8,128)S(1)} %bitcast.172, f32[1,32,32,128]{3,2,1,0:T(8,128)S(1)} %bitcast.174, f32[160,128]{1,0:T(8,128)S(1)} %get-tuple-element.5), kind=kOutput, calls=%fused_computation.18 | convolution fusion | flops 251953152 | bytes 1785856 | tf_op jit(solution)/shard_map/...nj,jc->...nc/dot_general | solution.py:86
  66.5 1.1 %add.210 = f32[1,1,32,4096]{3,2,1,0:T(8,128)S(1)} reshape(f32[32,32,128]{2,1,0:T(8,128)} %convolution_add_fusion.3) | data formatting | bytes 1048576 | tf_op jit(solution)/shard_map/add | solution.py:91
  67.9 1.9 %collective-permute-start.10 = (f32[2,1,16,4096]{3,2,1,0:T(8,128)S(1)}, f32[2,1,16,4096]{3,2,1,0:T(8,128)S(1)}, u32[]{:S(2)}, u32[]{:S(2)}) collective-permute-start(f32[2,1,16,4096]{3,2,1,0:T(8,128)S(1)} %get-tuple-element.14), channel_id=1, source_target_pairs={{1,0},{2,1},{3,2},{5,4},{6,5},{7,6},{9,8},{10,9},{11,10},{13,12},{... | collective-permute-start | bytes 1572872 | tf_op jit(solution)/shard_map/ppermute | solution.py:44
  69.8 3.9 %collective-permute-start.9 = (f32[2,1,16,4096]{3,2,1,0:T(8,128)S(1)}, f32[2,1,16,4096]{3,2,1,0:T(8,128)S(1)}, u32[]{:S(2)}, u32[]{:S(2)}) collective-permute-start(f32[2,1,16,4096]{3,2,1,0:T(8,128)S(1)} %get-tuple-element.13), channel_id=1, source_target_pairs={{0,1},{1,2},{2,3},{4,5},{5,6},{6,7},{8,9},{9,10},{10,11},{12,13},{... | collective-permute-start | bytes 1572872 | tf_op jit(solution)/shard_map/ppermute | solution.py:42
  73.7 4.7 %collective-permute-done.10 = f32[2,1,16,4096]{3,2,1,0:T(8,128)S(1)} collective-permute-done((f32[2,1,16,4096]{3,2,1,0:T(8,128)S(1)}, f32[2,1,16,4096]{3,2,1,0:T(8,128)S(1)}, u32[]{:S(2)}, u32[]{:S(2)}) %collective-permute-start.10) | collective-permute-done | bytes 524320 | tf_op jit(solution)/shard_map/ppermute | solution.py:44
  78.4 1.2 %collective-permute-done.9 = f32[2,1,16,4096]{3,2,1,0:T(8,128)S(1)} collective-permute-done((f32[2,1,16,4096]{3,2,1,0:T(8,128)S(1)}, f32[2,1,16,4096]{3,2,1,0:T(8,128)S(1)}, u32[]{:S(2)}, u32[]{:S(2)}) %collective-permute-start.9) | collective-permute-done | bytes 524320 | tf_op jit(solution)/shard_map/ppermute | solution.py:42
  82.3 1.0 %fusion.9 = f32[32,32,128]{2,1,0:T(8,128)S(1)} fusion(f32[1,32,32,32]{3,2,1,0:T(8,128)S(1)} %bitcast.167, f32[1,32,32,128]{3,2,1,0:T(8,128)S(1)} %bitcast.169, f32[160,128]{1,0:T(8,128)S(1)} %get-tuple-element.5), kind=kOutput, calls=%fused_computation.38 | convolution fusion | flops 251822080 | bytes 1261568 | tf_op jit(solution)/shard_map/...nj,jc->...nc/dot_general | solution.py:86
  83.3 1.0 %fusion.8 = f32[32,32,128]{2,1,0:T(8,128)S(1)} fusion(f32[1,32,32,32]{3,2,1,0:T(8,128)S(1)} %bitcast.168, f32[1,32,32,128]{3,2,1,0:T(8,128)S(1)} %bitcast.170, f32[160,128]{1,0:T(8,128)S(1)} %get-tuple-element.6), kind=kOutput, calls=%fused_computation.37 | convolution fusion | flops 251822080 | bytes 1261568 | tf_op jit(solution)/shard_map/...nj,jc->...nc/dot_general | solution.py:86
  85.5 1.0 %convolution_subtract_fusion.2 = f32[32,32,128]{2,1,0:T(8,128)S(1)} fusion(f32[32,32,128]{2,1,0:T(8,128)S(1)} %fusion.9, f32[1,32,32,32]{3,2,1,0:T(8,128)S(1)} %bitcast.175, f32[1,32,32,128]{3,2,1,0:T(8,128)S(1)} %bitcast.177, f32[160,128]{1,0:T(8,128)S(1)} %get-tuple-element.6), kind=kOutput, calls=%fused_computation.17 | convolution fusion | flops 251953152 | bytes 1785856 | tf_op jit(solution)/shard_map/...nj,jc->...nc/dot_general | solution.py:86
  86.6 1.0 %convolution_add_fusion.2 = f32[32,32,128]{2,1,0:T(8,128)S(1)} fusion(f32[32,32,128]{2,1,0:T(8,128)S(1)} %fusion.8, f32[1,32,32,32]{3,2,1,0:T(8,128)S(1)} %bitcast.176, f32[1,32,32,128]{3,2,1,0:T(8,128)S(1)} %bitcast.178, f32[160,128]{1,0:T(8,128)S(1)} %get-tuple-element.5), kind=kOutput, calls=%fused_computation.16 | convolution fusion | flops 251953152 | bytes 1785856 | tf_op jit(solution)/shard_map/...nj,jc->...nc/dot_general | solution.py:86
  87.7 1.0 %pad_maximum_fusion.2 = f32[2,1,32,4096]{3,2,1,0:T(8,128)} fusion(f32[1,1,32,4096]{3,2,1,0:T(8,128)S(1)} %add.216, f32[1,1,32,4096]{3,2,1,0:T(8,128)S(1)} %sub.201), kind=kLoop, calls=%fused_computation.32 | loop fusion | flops 262144 | bytes 2097152 | tf_op jit(solution)/shard_map/stack | solution.py:150
  (64 shorter events, 17.0 us)
Async XLA Ops:
  0.0 8.5 %collective-permute-start = (f32[2,32,512]{2,1,0:T(8,128)}, f32[2,32,512]{2,1,0:T(8,128)S(1)}, u32[]{:S(2)}, u32[]{:S(2)}) collective-permute-start(f32[2,32,512]{2,1,0:T(8,128)} %param.6), channel_id=1, source_target_pairs={{0,4},{4,8},{8,12},{12,16},{16,20},{20,24},{24,28},{28,0},{1,5},{5... | collective-permute-start | bytes 393224 | tf_op jit(solution)/shard_map/ppermute | solution.py:25
  2.1 14.3 %collective-permute-start.4 = (f32[2,32,512]{2,1,0:T(8,128)}, f32[2,32,512]{2,1,0:T(8,128)S(1)}, u32[]{:S(2)}, u32[]{:S(2)}) collective-permute-start(f32[2,32,512]{2,1,0:T(8,128)} %param.6), channel_id=1, source_target_pairs={{4,0},{8,4},{12,8},{16,12},{20,16},{24,20},{28,24},{0,28},{5,1},{9... | collective-permute-start | bytes 393224 | tf_op jit(solution)/shard_map/ppermute | solution.py:27
  8.5 6.5 %collective-permute-start.1 = (f32[2,32,512]{2,1,0:T(8,128)S(1)}, f32[2,32,512]{2,1,0:T(8,128)S(1)}, u32[]{:S(2)}, u32[]{:S(2)}) collective-permute-start(f32[2,32,512]{2,1,0:T(8,128)S(1)} %collective-permute-done), channel_id=1, source_target_pairs={{0,4},{4,8},{8,12},{12,16},{16,20},{20,24},{24,28},{28,0},{1,5},{5... | collective-permute-start | bytes 393224 | tf_op jit(solution)/shard_map/ppermute | solution.py:25
  15.1 6.6 %collective-permute-start.2 = (f32[2,32,512]{2,1,0:T(8,128)S(1)}, f32[2,32,512]{2,1,0:T(8,128)S(1)}, u32[]{:S(2)}, u32[]{:S(2)}) collective-permute-start(f32[2,32,512]{2,1,0:T(8,128)S(1)} %collective-permute-done.1), channel_id=1, source_target_pairs={{0,4},{4,8},{8,12},{12,16},{16,20},{20,24},{24,28},{28,0},{1,5},{5... | collective-permute-start | bytes 393224 | tf_op jit(solution)/shard_map/ppermute | solution.py:25
  16.4 6.2 %collective-permute-start.5 = (f32[2,32,512]{2,1,0:T(8,128)S(1)}, f32[2,32,512]{2,1,0:T(8,128)S(1)}, u32[]{:S(2)}, u32[]{:S(2)}) collective-permute-start(f32[2,32,512]{2,1,0:T(8,128)S(1)} %collective-permute-done.4), channel_id=1, source_target_pairs={{4,0},{8,4},{12,8},{16,12},{20,16},{24,20},{28,24},{0,28},{5,1},{9... | collective-permute-start | bytes 393224 | tf_op jit(solution)/shard_map/ppermute | solution.py:27
  21.7 6.5 %collective-permute-start.3 = (f32[2,32,512]{2,1,0:T(8,128)S(1)}, f32[2,32,512]{2,1,0:T(8,128)S(1)}, u32[]{:S(2)}, u32[]{:S(2)}) collective-permute-start(f32[2,32,512]{2,1,0:T(8,128)S(1)} %collective-permute-done.2), channel_id=1, source_target_pairs={{0,4},{4,8},{8,12},{12,16},{16,20},{20,24},{24,28},{28,0},{1,5},{5... | collective-permute-start | bytes 393224 | tf_op jit(solution)/shard_map/ppermute | solution.py:25
  22.5 6.7 %collective-permute-start.6 = (f32[2,32,512]{2,1,0:T(8,128)S(1)}, f32[2,32,512]{2,1,0:T(8,128)S(1)}, u32[]{:S(2)}, u32[]{:S(2)}) collective-permute-start(f32[2,32,512]{2,1,0:T(8,128)S(1)} %collective-permute-done.5), channel_id=1, source_target_pairs={{4,0},{8,4},{12,8},{16,12},{20,16},{24,20},{28,24},{0,28},{5,1},{9... | collective-permute-start | bytes 393224 | tf_op jit(solution)/shard_map/ppermute | solution.py:27
  36.3 14.2 %collective-permute-start.7 = (f32[2,1,16,4096]{3,2,1,0:T(8,128)}, f32[2,1,16,4096]{3,2,1,0:T(8,128)}, u32[]{:S(2)}, u32[]{:S(2)}) collective-permute-start(f32[2,1,16,4096]{3,2,1,0:T(8,128)} %get-tuple-element.17), channel_id=1, source_target_pairs={{0,1},{1,2},{2,3},{4,5},{5,6},{6,7},{8,9},{9,10},{10,11},{12,13},{... | collective-permute-start | bytes 1572872 | tf_op jit(solution)/shard_map/ppermute | solution.py:42
  44.1 10.6 %collective-permute-start.8 = (f32[2,1,16,4096]{3,2,1,0:T(8,128)S(1)}, f32[2,1,16,4096]{3,2,1,0:T(8,128)}, u32[]{:S(2)}, u32[]{:S(2)}) collective-permute-start(f32[2,1,16,4096]{3,2,1,0:T(8,128)S(1)} %get-tuple-element.18), channel_id=1, source_target_pairs={{1,0},{2,1},{3,2},{5,4},{6,5},{7,6},{9,8},{10,9},{11,10},{13,12},{... | collective-permute-start | bytes 1572872 | tf_op jit(solution)/shard_map/ppermute | solution.py:44
  67.9 10.5 %collective-permute-start.10 = (f32[2,1,16,4096]{3,2,1,0:T(8,128)S(1)}, f32[2,1,16,4096]{3,2,1,0:T(8,128)S(1)}, u32[]{:S(2)}, u32[]{:S(2)}) collective-permute-start(f32[2,1,16,4096]{3,2,1,0:T(8,128)S(1)} %get-tuple-element.14), channel_id=1, source_target_pairs={{1,0},{2,1},{3,2},{5,4},{6,5},{7,6},{9,8},{10,9},{11,10},{13,12},{... | collective-permute-start | bytes 1572872 | tf_op jit(solution)/shard_map/ppermute | solution.py:44
  69.8 9.8 %collective-permute-start.9 = (f32[2,1,16,4096]{3,2,1,0:T(8,128)S(1)}, f32[2,1,16,4096]{3,2,1,0:T(8,128)S(1)}, u32[]{:S(2)}, u32[]{:S(2)}) collective-permute-start(f32[2,1,16,4096]{3,2,1,0:T(8,128)S(1)} %get-tuple-element.13), channel_id=1, source_target_pairs={{0,1},{1,2},{2,3},{4,5},{5,6},{6,7},{8,9},{9,10},{10,11},{12,13},{... | collective-permute-start | bytes 1572872 | tf_op jit(solution)/shard_map/ppermute | solution.py:42
